TPU v7x, 256 devices: a whole 4x4x8 slice. The times are simulated.
256 devices in a mesh: group: 2 (over core), dp: 16 (over y, x), tensor: 8 (over z).
Axes of the slice: x: 4, y: 4, z: 8, core: 2. Of those that a mesh axis runs over, the one named last changes fastest.
Arguments:
- stream: bfloat16 [512, 8192], P('tensor', ('group', 'dp'))
- norm_attn: bfloat16 [8192], P(('group', 'dp')), may hold values from 0.29882812 to 3
- norm_ffn: bfloat16 [8192], P(('group', 'dp')), may hold values from 0.29882812 to 3
- w_query: bfloat16 [8192, 8192], P(('group', 'dp'), 'tensor'), may hold values from -0.0625 to 0.0625
- w_keyval: bfloat16 [8192, 2048], P(('group', 'dp'), 'tensor'), may hold values from -0.0625 to 0.0625
- w_out: bfloat16 [8192, 8192], P('tensor', ('group', 'dp')), may hold values from -0.0625 to 0.0625
- w_gate: bfloat16 [8192, 28672], P(('group', 'dp'), 'tensor'), may hold values from -0.0625 to 0.0625
- w_up: bfloat16 [8192, 28672], P(('group', 'dp'), 'tensor'), may hold values from -0.0625 to 0.0625
- w_down: bfloat16 [28672, 8192], P('tensor', ('group', 'dp')), may hold values from -0.03125 to 0.03125
- cache: bfloat16 [512, 8, 256, 256], P(('group', 'dp'), 'tensor')
- lengths: int32 [512], P(('group', 'dp')), may hold values from 1 to 256, as said below
- location: int32 [512], P(('group', 'dp')), may hold values from 0 to 511, as said below
Outputs:
- updated: float32 [512, 8192], P('tensor', ('group', 'dp'))
Inputs may be any that keep to these rules, and one draw needn't show every extreme that they name: Each of the 512 slots is named by exactly one request. Slot s belongs to owner s // 16. Requests r of one aligned block of 16 (one device's requests) that share an owner have different values of location modulo 2; in every draw 2 of them share an owner. `lengths`: some slot holds 256 valid positions in every draw.
All inputs are finite; a program needn't handle non-finite values.
Results may differ from a plain program's by a relative error of at most 0.005.
The roundings to bfloat16 on the way count: a program that leaves them out, or rounds other values in their place, can miss the bound.
Values may be sent and summed in bfloat16 or wider, within the bound.
No kernel may reach another device: no remote copies, remote signals or barrier semaphores. Data moves between devices by JAX's collectives and lax.ppermute only.
A program may use at most 64 MiB of HBM per device.

v0:
```python
import jax
import jax.numpy as jnp
from jax import lax
from jax.sharding import PartitionSpec as P

D = 8192
CAP = 2
EPSILON = 1e-05


def normed(values, gain):
    squares = lax.psum(jnp.sum(values * values, axis=1), ("group", "dp"))
    scale = lax.rsqrt(squares / D + EPSILON)
    return (values * scale[:, None] * gain.astype(jnp.float32)[None, :]).astype(jnp.bfloat16)


def width_sum(normal_rows, matrices):
    gathered = lax.all_gather(normal_rows, "tensor", axis=0, tiled=True)
    return lax.psum_scatter(
        jnp.concatenate(
            [jnp.dot(gathered, matrix, preferred_element_type=jnp.float32) for matrix in matrices],
            axis=1,
        ),
        ("group", "dp"),
        scatter_dimension=0,
        tiled=True,
    )


def project_rows(local_rows, matrix):
    partial_sum = jnp.dot(
        lax.all_gather(local_rows, ("group", "dp"), axis=0, tiled=True),
        matrix,
        preferred_element_type=jnp.float32,
    )
    return lax.psum_scatter(partial_sum, "tensor", scatter_dimension=0, tiled=True)


def attend(query, fresh, stored, counts):
    items = query.shape[0]
    kv_local = stored.shape[1]
    head_size = stored.shape[3] // 2
    grouped = query.reshape(items, kv_local, -1, head_size)
    fresh = fresh.reshape(items, kv_local, 2 * head_size)
    scale = head_size ** (-0.5)
    scores = (
        jnp.einsum(
            "mkgd,mkpd->mkgp", grouped, stored[..., :head_size], preferred_element_type=jnp.float32
        )
        * scale
    )
    own = (
        jnp.einsum(
            "mkgd,mkd->mkg", grouped, fresh[..., :head_size], preferred_element_type=jnp.float32
        )
        * scale
    )
    place = jnp.arange(stored.shape[2], dtype=jnp.int32)
    valid = place[None, None, None, :] < counts[:, None, None, None]
    top = jnp.maximum(jnp.max(jnp.where(valid, scores, -1e30), axis=3), own)
    expo = jnp.where(valid, jnp.exp(scores - top[..., None]), 0.0)
    own_expo = jnp.exp(own - top)
    total = jnp.sum(expo, axis=3) + own_expo
    probs = (expo / total[..., None]).astype(jnp.bfloat16)
    own_prob = (own_expo / total).astype(jnp.bfloat16)
    mixed = jnp.einsum(
        "mkgp,mkpd->mkgd", probs, stored[..., head_size:], preferred_element_type=jnp.float32
    )
    mixed = mixed + own_prob.astype(jnp.float32)[..., None] * fresh[:, :, None, head_size:].astype(
        jnp.float32
    )
    return mixed.reshape(items, -1).astype(jnp.bfloat16)


def per_device(
    stream,
    norm_attn,
    norm_ffn,
    w_query,
    w_keyval,
    w_out,
    w_gate,
    w_up,
    w_down,
    cache,
    lengths,
    location,
):
    owners = lax.axis_size(("group", "dp"))
    per_owner = cache.shape[0]
    resid = stream.astype(jnp.float32)
    attn_in = normed(resid, norm_attn)
    joined = width_sum(attn_in, (w_query, w_keyval))
    query_cols = w_query.shape[1]
    query = joined[:, :query_cols].astype(jnp.bfloat16)
    fresh = joined[:, query_cols:].astype(jnp.bfloat16)
    fresh_cols = fresh.shape[1]
    target = location // per_owner
    place = target * CAP + location % per_owner % CAP
    slot = location % per_owner
    send_query = (
        jnp.zeros((owners * CAP, query_cols), jnp.bfloat16)
        .at[place]
        .set(query)
        .reshape(owners, CAP, query_cols)
    )
    send_fresh = (
        jnp.zeros((owners * CAP, fresh_cols), jnp.bfloat16)
        .at[place]
        .set(fresh)
        .reshape(owners, CAP, fresh_cols)
    )
    send_slot = jnp.zeros((owners * CAP,), jnp.int32).at[place].set(slot).reshape(owners, CAP)
    got_query = lax.all_to_all(send_query, ("group", "dp"), split_axis=0, concat_axis=0, tiled=True)
    got_fresh = lax.all_to_all(send_fresh, ("group", "dp"), split_axis=0, concat_axis=0, tiled=True)
    got_slot = lax.all_to_all(send_slot, ("group", "dp"), split_axis=0, concat_axis=0, tiled=True)
    sources = got_slot.shape[0]
    count = got_slot.shape[1]
    flat_slot = got_slot.reshape(-1)
    answer = attend(
        got_query.reshape(sources * count, -1),
        got_fresh.reshape(sources * count, -1),
        cache[flat_slot],
        lengths[flat_slot],
    )
    answer = answer.reshape(sources, count, -1)
    returned = lax.all_to_all(answer, ("group", "dp"), split_axis=0, concat_axis=0, tiled=True)
    attended = returned.reshape(owners * CAP, -1)[place]
    middle = resid + project_rows(attended, w_out)
    ffn_in = normed(middle, norm_ffn)
    both = width_sum(ffn_in, (w_gate, w_up))
    hidden_cols = w_gate.shape[1]
    hidden = (jax.nn.silu(both[:, :hidden_cols]) * both[:, hidden_cols:]).astype(jnp.bfloat16)
    return middle + project_rows(hidden, w_down)


def solution(mesh):
    placed = (
        P("tensor", ("group", "dp")),
        P(("group", "dp")),
        P(("group", "dp")),
        P(("group", "dp"), "tensor"),
        P(("group", "dp"), "tensor"),
        P("tensor", ("group", "dp")),
        P(("group", "dp"), "tensor"),
        P(("group", "dp"), "tensor"),
        P("tensor", ("group", "dp")),
        P(("group", "dp"), "tensor", None, None),
        P(("group", "dp")),
        P(("group", "dp")),
    )
    return jax.shard_map(
        per_device,
        mesh=mesh,
        in_specs=placed,
        out_specs=P("tensor", ("group", "dp")),
        check_vma=False,
    )
```

profile of v0, /device:TPU:6, one launch (start us, length us, event | category | flops | bytes accessed | tf_op | source)
XLA Modules:
  0.0 643.8 jit_solution(16838073562884392161)
XLA Ops:
  6.5 1.0 fusion.11
  7.6 62.1 %psum.14 = f32[64]{0:T(128)S(1)} all-reduce(f32[64]{0:T(128)S(1)} %fusion.11), channel_id=1, replica_groups=mesh['group'=2,'dp'=16,'tensor'=8] {'group','dp'}, use_global_device_ids=true, to_apply=%region_2.0 | all-reduce | flops 64 | bytes 512 | tf_op jit(solution)/shard_map/psum | solution.py:12
  69.6 0.7 convert_element_type.51
  70.3 0.8 fusion.13
  71.1 26.8 %all_gather.12 = bf16[512,256]{1,0:T(8,128)(2,1)S(1)} all-gather(bf16[64,256]{1,0:T(8,128)(2,1)S(1)} %fusion.13), channel_id=1, replica_groups=mesh['group'=2,'dp'=16,'tensor'=8] {'tensor'}, dimensions={0}, use_global_device_ids=true | all-gather | bytes 294912 | tf_op jit(solution)/shard_map/all_gather | solution.py:18
  98.0 1.1 fusion.33
  99.1 1.5 fusion.32
  100.6 1.7 pad_maximum_fusion.1
  102.4 0.6 scatter_custom_fusion
  103.1 15.8 %all_to_all.24 = s32[32,1,2]{2,1,0:T(1,128)S(1)} all-to-all(s32[32,1,2]{2,1,0:T(1,128)S(1)} %bitcast.51), channel_id=1, replica_groups=mesh['group'=2,'dp'=16,'tensor'=8] {'group','dp'}, dimensions={0} | all-to-all | bytes 512 | tf_op jit(solution)/shard_map/all_to_all | solution.py:116
  119.0 0.5 broadcast.136
  119.5 0.7 reduce.7
  120.2 0.1 reshape.143
  120.3 0.8 gather_fusion
  121.1 69.7 %reduce-scatter.5.cloned.1.call-done = f32[16,1280]{1,0:T(8,128)} async-done(((f32[512,1280]{1,0:T(8,128)}), f32[16,1280]{1,0:T(8,128)}) %reduce-scatter.5.cloned.1.call-update) | async-done | bytes 81936 | tf_op jit(solution)/shard_map/reduce_scatter | solution.py:19
  190.8 0.9 convert.5
  191.7 0.7 scatter_custom_fusion.2
  192.4 0.6 reshape.147
  193.0 5.9 all-to-all-start.2
  199.0 5.3 gather_fusion.1
  204.3 0.7 scatter_custom_fusion.1
  205.1 0.7 reshape.144
  205.8 7.4 %all-to-all-start.1 = ((bf16[32,2,1024]{2,1,0:T(2,128)(2,1)}), bf16[32,2,1024]{2,1,0:T(2,128)(2,1)S(1)}, u32[]{:S(2)}, u32[]{:S(2)}) async-start(bf16[32,2,1024]{2,1,0:T(2,128)(2,1)} %reshape.144), calls=%async_computation.2 | async-start | bytes 262144 | tf_op jit(solution)/shard_map/all_to_all | solution.py:114
  213.2 6.3 all-to-all-done.1
  219.6 0.2 fusion.17
  219.8 3.5 select_reduce_fusion
  223.3 0.3 fusion.5
  223.6 3.0 fusion.4
  226.6 0.7 convert_element_type.59
  227.3 5.2 all-to-all-start.3
  232.6 6.4 all-to-all-done.3
  239.0 1.2 gather_fusion.2
  240.3 46.3 %all-gather.6.cloned.1.call-done = bf16[512,1024]{1,0:T(8,128)(2,1)} async-done(((bf16[16,1024]{1,0:T(8,128)(2,1)}), bf16[512,1024]{1,0:T(8,128)(2,1)}) %all-gather.6.cloned.1.call-update) | async-done | bytes 1048592 | tf_op jit(solution)/shard_map/all_gather | solution.py:32
  286.6 2.5 fusion.34
  289.2 37.6 %reduce-scatter.7.cloned.1.call-done = f32[64,256]{1,0:T(8,128)} async-done(((f32[512,256]{1,0:T(8,128)}), f32[64,256]{1,0:T(8,128)}) %reduce-scatter.7.cloned.1.call-update) | async-done | bytes 65552 | tf_op jit(solution)/shard_map/reduce_scatter | solution.py:36
  326.8 0.9 multiply_reduce_fusion
  327.7 60.4 %psum.15 = f32[64]{0:T(128)S(1)} all-reduce(f32[64]{0:T(128)S(1)} %multiply_reduce_fusion), channel_id=1, replica_groups=mesh['group'=2,'dp'=16,'tensor'=8] {'group','dp'}, use_global_device_ids=true, to_apply=%region_10.11 | all-reduce | flops 64 | bytes 512 | tf_op jit(solution)/shard_map/psum | solution.py:12
  388.2 0.9 multiply_convert_fusion
  389.1 24.9 %all_gather.14 = bf16[512,256]{1,0:T(8,128)(2,1)S(1)} all-gather(bf16[64,256]{1,0:T(8,128)(2,1)S(1)} %multiply_convert_fusion), channel_id=1, replica_groups=mesh['group'=2,'dp'=16,'tensor'=8] {'tensor'}, dimensions={0}, use_global_device_ids=true | all-gather | bytes 294912 | tf_op jit(solution)/shard_map/all_gather | solution.py:18
  414.0 2.8 fusion.36
  416.7 1.1 fusion.35
  417.8 5.5 pad_maximum_fusion
  423.4 117.5 %reduce-scatter.9.cloned.1.call-done = f32[16,7168]{1,0:T(8,128)} async-done(((f32[512,7168]{1,0:T(8,128)}), f32[16,7168]{1,0:T(8,128)}) %reduce-scatter.9.cloned.1.call-update) | async-done | bytes 458768 | tf_op jit(solution)/shard_map/reduce_scatter | solution.py:19
  540.9 1.8 fusion.10
  542.7 50.4 %all-gather.4.cloned.1.call-done = bf16[512,3584]{1,0:T(8,128)(2,1)} async-done(((bf16[16,3584]{1,0:T(8,128)(2,1)}), bf16[512,3584]{1,0:T(8,128)(2,1)}) %all-gather.4.cloned.1.call-update) | async-done | bytes 3670032 | tf_op jit(solution)/shard_map/all_gather | solution.py:32
  593.1 4.5 fusion.37
  597.7 37.7 %reduce-scatter.11.cloned.1.call-done = f32[64,256]{1,0:T(8,128)} async-done(((f32[512,256]{1,0:T(8,128)}), f32[64,256]{1,0:T(8,128)}) %reduce-scatter.11.cloned.1.call-update) | async-done | bytes 65552 | tf_op jit(solution)/shard_map/reduce_scatter | solution.py:36
  635.4 1.5 fusion.19
  (44 shorter events, 0.8 us)
Async XLA Ops:
  6.5 192.5 %copy-start = (bf16[16,1,256,256]{3,2,1,0:T(8,128)(2,1)S(1)}, bf16[16,1,256,256]{3,2,1,0:T(8,128)(2,1)}, u32[]{:S(2)}) copy-start(bf16[16,1,256,256]{3,2,1,0:T(8,128)(2,1)} %param.21) | copy-start | bytes 6291460
  6.5 184.3 %reduce-scatter.5.cloned.1.call-start = ((), (), s32[]{:S(2)}) async-start(), calls=%async_computation.8 | async-start | bytes 2703360 | tf_op jit(solution)/shard_map/reduce_scatter | solution.py:19
  100.6 1.8 copy-start.6
  100.6 19.7 %copy-start.1 = (s32[16]{0:T(128)S(1)}, s32[16]{0:T(128)}, u32[]{:S(2)}) copy-start(s32[16]{0:T(128)} %param.22) | copy-start | bytes 196
  193.0 12.8 %all-to-all-start.2 = ((bf16[32,2,256]{2,1,0:T(2,128)(2,1)}), bf16[32,2,256]{2,1,0:T(2,128)(2,1)S(1)}, u32[]{:S(2)}, u32[]{:S(2)}) async-start(bf16[32,2,256]{2,1,0:T(2,128)(2,1)} %reshape.147), calls=%async_computation.3 | async-start | bytes 65536 | tf_op jit(solution)/shard_map/all_to_all | solution.py:115
  205.8 13.7 %all-to-all-start.1 = ((bf16[32,2,1024]{2,1,0:T(2,128)(2,1)}), bf16[32,2,1024]{2,1,0:T(2,128)(2,1)S(1)}, u32[]{:S(2)}, u32[]{:S(2)}) async-start(bf16[32,2,1024]{2,1,0:T(2,128)(2,1)} %reshape.144), calls=%async_computation.2 | async-start | bytes 262144 | tf_op jit(solution)/shard_map/all_to_all | solution.py:114
  223.6 63.0 %copy-start.5 = (bf16[1024,256]{1,0:T(8,128)(2,1)S(1)}, bf16[1024,256]{1,0:T(8,128)(2,1)}, u32[]{:S(2)}) copy-start(bf16[1024,256]{1,0:T(8,128)(2,1)} %param.17) | copy-start | bytes 1572868
  223.6 65.6 %copy-start.7 = (bf16[256]{0:T(256)(128)(2,1)S(1)}, bf16[256]{0:T(256)(128)(2,1)}, u32[]{:S(2)}) copy-start(bf16[256]{0:T(256)(128)(2,1)} %param.14) | copy-start | bytes 1540
  223.6 103.2 %copy-start.3 = (bf16[64,256]{1,0:T(8,128)(2,1)S(1)}, bf16[64,256]{1,0:T(8,128)(2,1)}, u32[]{:S(2)}) copy-start(bf16[64,256]{1,0:T(8,128)(2,1)} %param.12) | copy-start | bytes 98308
  227.3 11.7 %all-to-all-start.3 = ((bf16[32,2,1024]{2,1,0:T(2,128)(2,1)}), bf16[32,2,1024]{2,1,0:T(2,128)(2,1)S(1)}, u32[]{:S(2)}, u32[]{:S(2)}) async-start(bf16[32,2,1024]{2,1,0:T(2,128)(2,1)} %convert_element_type.59), calls=%async_computation.4 | async-start | bytes 262144 | tf_op jit(solution)/shard_map/all_to_all | solution.py:127
  232.5 54.0 %all-gather.6.cloned.1.call-start = ((), (), s32[]{:S(2)}) async-start(), calls=%async_computation.13 | async-start | bytes 1081344 | tf_op jit(solution)/shard_map/all_gather | solution.py:32
  240.3 86.5 %reduce-scatter.7.cloned.1.call-start = ((), (), s32[]{:S(2)}) async-start(), calls=%async_computation.9 | async-start | bytes 589824 | tf_op jit(solution)/shard_map/reduce_scatter | solution.py:36
  289.1 251.8 %reduce-scatter.9.cloned.1.call-start = ((), (), s32[]{:S(2)}) async-start(), calls=%async_computation.10 | async-start | bytes 15138816 | tf_op jit(solution)/shard_map/reduce_scatter | solution.py:19
  414.0 2.8 copy-start.2
  423.4 169.8 %all-gather.4.cloned.1.call-start = ((), (), s32[]{:S(2)}) async-start(), calls=%async_computation.11 | async-start | bytes 3784704 | tf_op jit(solution)/shard_map/all_gather | solution.py:32
  542.7 92.8 %copy-start.4 = (f32[64,256]{1,0:T(8,128)S(1)}, f32[64,256]{1,0:T(8,128)}, u32[]{:S(2)}) copy-start(f32[64,256]{1,0:T(8,128)} %reduce-scatter.7.cloned.1.call-done) | copy-start | bytes 196612
  542.7 92.8 %reduce-scatter.11.cloned.1.call-start = ((), (), s32[]{:S(2)}) async-start(), calls=%async_computation.12 | async-start | bytes 589824 | tf_op jit(solution)/shard_map/reduce_scatter | solution.py:36
Sparse Core Ops, SparseCore 0:
  102.5 88.2 reduce-scatter.4
  240.4 46.1 all-gather.5
  289.2 37.5 reduce-scatter.6
  423.5 117.3 reduce-scatter.8
  543.3 49.8 all-gather.3
  597.8 37.5 reduce-scatter.10
where the time goes:
time: 645 us; the launch traced here: 644 us
  waiting for transfers between devices  372 us (58%)
  blocking collectives  190 us (29%)
  matrix products  20.1 us (3%)
  starting transfers between devices  18.7 us (3%)
  other arithmetic  16.8 us (3%)
  between operations  13.8 us (2%)
  local copies, waits for them, and re-layouts  12.3 us (2%)
    reduce_scatter x2, waiting for transfers between devices, width_sum(): lax.psum_scatter(jnp.concatenate([jnp.dot(gathered, matrix, preferred_ele...  187 us
    psum x2, blocking collectives, normed(): squares = lax.psum(jnp.sum(values * values, axis=1), ('group', 'dp'))  123 us
    all_gather x2, waiting for transfers between devices, project_rows(): lax.all_gather(local_rows, ('group', 'dp'), axis=0, tiled=True)  96.7 us
    reduce_scatter x2, waiting for transfers between devices, project_rows(): lax.psum_scatter(partial_sum, 'tensor', scatter_dimension=0, tiled=True)  75.4 us
    all_gather x2, blocking collectives, width_sum(): gathered = lax.all_gather(normal_rows, 'tensor', axis=0, tiled=True)  51.7 us
    all_to_all x1, blocking collectives, per_device(): lax.all_to_all(send_slot, ('group', 'dp'), split_axis=0, concat_axis=0, t...  15.8 us
  transfers between devices with their start and end apart: 9, of which 8 were waited for; matrix products, arithmetic and copies ran while one was open for 1% of the time, Pallas kernels for 0%

commit v1 on v0

--- a/solution.py
+++ b/solution.py
@@ -15,7 +15,10 @@
 
 
 def width_sum(normal_rows, matrices):
-    gathered = lax.all_gather(normal_rows, "tensor", axis=0, tiled=True)
+    peers = lax.axis_size("tensor")
+    blocks = jnp.stack([normal_rows for _ in range(peers)])
+    blocks = lax.all_to_all(blocks, "tensor", split_axis=0, concat_axis=0)
+    gathered = jnp.concatenate(blocks, axis=0)
     return lax.psum_scatter(
         jnp.concatenate(
             [jnp.dot(gathered, matrix, preferred_element_type=jnp.float32) for matrix in matrices],

time: 645 us -> 621 us (0.963)
  blocking collectives: 190 us -> 172 us
    all_gather x2 -> x0, blocking collectives: 51.7 us -> none  [width_sum(): gathered = lax.all_gather(normal_rows, 'tensor', axis=0, tiled=True)]
    all_to_all x0 -> x2, blocking collectives: none -> 31.8 us  [width_sum(): blocks = lax.all_to_all(blocks, 'tensor', split_axis=0, concat_axis=0)]
  transfers between devices with their start and end apart: 9 -> 9, of which waited for: 8 -> 8; matrix products, arithmetic and copies ran while one was open for 1% -> 2% of each run, Pallas kernels for 0% -> 0%
where the time goes in v1:
time: 621 us; the launch traced here: 620 us
  waiting for transfers between devices  367 us (59%)
  blocking collectives  172 us (28%)
  matrix products  20.1 us (3%)
  starting transfers between devices  18.7 us (3%)
  other arithmetic  16.8 us (3%)
  between operations  13.8 us (2%)
  local copies, waits for them, and re-layouts  12.3 us (2%)
    reduce_scatter x2, waiting for transfers between devices, width_sum(): lax.psum_scatter(jnp.concatenate([jnp.dot(gathered, matrix, preferred_ele...  182 us
    psum x2, blocking collectives, normed(): squares = lax.psum(jnp.sum(values * values, axis=1), ('group', 'dp'))  123 us
    all_gather x2, waiting for transfers between devices, project_rows(): lax.all_gather(local_rows, ('group', 'dp'), axis=0, tiled=True)  96.7 us
    reduce_scatter x2, waiting for transfers between devices, project_rows(): lax.psum_scatter(partial_sum, 'tensor', scatter_dimension=0, tiled=True)  75.4 us
    all_to_all x2, blocking collectives, width_sum(): blocks = lax.all_to_all(blocks, 'tensor', split_axis=0, concat_axis=0)  31.8 us
    all_to_all x1, blocking collectives, per_device(): lax.all_to_all(send_slot, ('group', 'dp'), split_axis=0, concat_axis=0, t...  17.7 us
  transfers between devices with their start and end apart: 9, of which 8 were waited for; matrix products, arithmetic and copies ran while one was open for 2% of the time, Pallas kernels for 0%

profile of v1, /device:TPU:6, one launch (start us, length us, event | category | flops | bytes accessed | tf_op | source)
XLA Modules:
  0.0 620.3 jit_solution(16713877027920137040)
XLA Ops:
  6.5 1.0 fusion.11
  7.6 62.1 %psum.14 = f32[64]{0:T(128)S(1)} all-reduce(f32[64]{0:T(128)S(1)} %fusion.11), channel_id=1, replica_groups=mesh['group'=2,'dp'=16,'tensor'=8] {'group','dp'}, use_global_device_ids=true, to_apply=%region_2.0 | all-reduce | flops 64 | bytes 512 | tf_op jit(solution)/shard_map/psum | solution.py:12
  69.6 0.7 convert_element_type.51
  70.3 0.8 fusion.13
  71.2 17.3 %all_to_all.34 = bf16[8,64,256]{2,1,0:T(8,128)(2,1)S(1)} all-to-all(bf16[8,64,256]{2,1,0:T(8,128)(2,1)S(1)} %stack.4), channel_id=1, replica_groups=mesh['group'=2,'dp'=16,'tensor'=8] {'tensor'}, dimensions={0} | all-to-all | bytes 524288 | tf_op jit(solution)/shard_map/all_to_all | solution.py:20
  88.5 1.1 fusion.33
  89.6 1.5 fusion.32
  91.1 1.7 pad_maximum_fusion.1
  92.9 0.6 scatter_custom_fusion
  93.6 17.7 %all_to_all.35 = s32[32,1,2]{2,1,0:T(1,128)S(1)} all-to-all(s32[32,1,2]{2,1,0:T(1,128)S(1)} %bitcast.57), channel_id=1, replica_groups=mesh['group'=2,'dp'=16,'tensor'=8] {'group','dp'}, dimensions={0} | all-to-all | bytes 512 | tf_op jit(solution)/shard_map/all_to_all | solution.py:119
  111.3 0.5 broadcast.140
  111.8 0.7 reduce.7
  112.5 0.1 reshape.153
  112.6 0.8 gather_fusion
  113.4 66.7 %reduce-scatter.5.cloned.1.call-done = f32[16,1280]{1,0:T(8,128)} async-done(((f32[512,1280]{1,0:T(8,128)}), f32[16,1280]{1,0:T(8,128)}) %reduce-scatter.5.cloned.1.call-update) | async-done | bytes 81936 | tf_op jit(solution)/shard_map/reduce_scatter | solution.py:22
  180.1 0.9 convert.5
  181.0 0.7 scatter_custom_fusion.2
  181.7 0.6 reshape.158
  182.3 5.8 all-to-all-start.3
  188.3 5.3 gather_fusion.1
  193.6 0.7 scatter_custom_fusion.1
  194.4 0.7 reshape.155
  195.1 7.4 %all-to-all-start.2 = ((bf16[32,2,1024]{2,1,0:T(2,128)(2,1)}), bf16[32,2,1024]{2,1,0:T(2,128)(2,1)S(1)}, u32[]{:S(2)}, u32[]{:S(2)}) async-start(bf16[32,2,1024]{2,1,0:T(2,128)(2,1)} %reshape.155), calls=%async_computation.3 | async-start | bytes 262144 | tf_op jit(solution)/shard_map/all_to_all | solution.py:117
  202.5 6.3 %all-to-all-done.2 = bf16[32,2,1024]{2,1,0:T(2,128)(2,1)S(1)} async-done(((bf16[32,2,1024]{2,1,0:T(2,128)(2,1)}), bf16[32,2,1024]{2,1,0:T(2,128)(2,1)S(1)}, u32[]{:S(2)}, u32[]{:S(2)}) %all-to-all-start.2) | async-done | bytes 131104 | tf_op jit(solution)/shard_map/all_to_all | solution.py:117
  208.9 0.2 fusion.17
  209.1 3.5 select_reduce_fusion
  212.6 0.3 fusion.5
  212.9 3.0 fusion.4
  215.9 0.7 convert_element_type.59
  216.6 5.2 all-to-all-start.4
  221.9 6.4 %all-to-all-done.4 = bf16[32,2,1024]{2,1,0:T(2,128)(2,1)S(1)} async-done(((bf16[32,2,1024]{2,1,0:T(2,128)(2,1)}), bf16[32,2,1024]{2,1,0:T(2,128)(2,1)S(1)}, u32[]{:S(2)}, u32[]{:S(2)}) %all-to-all-start.4) | async-done | bytes 131104 | tf_op jit(solution)/shard_map/all_to_all | solution.py:130
  228.3 1.2 gather_fusion.2
  229.6 46.3 %all-gather.6.cloned.1.call-done = bf16[512,1024]{1,0:T(8,128)(2,1)} async-done(((bf16[16,1024]{1,0:T(8,128)(2,1)}), bf16[512,1024]{1,0:T(8,128)(2,1)}) %all-gather.6.cloned.1.call-update) | async-done | bytes 1048592 | tf_op jit(solution)/shard_map/all_gather | solution.py:35
  275.9 2.5 fusion.34
  278.4 37.6 %reduce-scatter.7.cloned.1.call-done = f32[64,256]{1,0:T(8,128)} async-done(((f32[512,256]{1,0:T(8,128)}), f32[64,256]{1,0:T(8,128)}) %reduce-scatter.7.cloned.1.call-update) | async-done | bytes 65552 | tf_op jit(solution)/shard_map/reduce_scatter | solution.py:39
  316.1 0.9 multiply_reduce_fusion
  317.0 60.4 %psum.15 = f32[64]{0:T(128)S(1)} all-reduce(f32[64]{0:T(128)S(1)} %multiply_reduce_fusion), channel_id=1, replica_groups=mesh['group'=2,'dp'=16,'tensor'=8] {'group','dp'}, use_global_device_ids=true, to_apply=%region_10.11 | all-reduce | flops 64 | bytes 512 | tf_op jit(solution)/shard_map/psum | solution.py:12
  377.5 0.9 multiply_convert_fusion
  378.4 14.5 %all_to_all.36 = bf16[8,64,256]{2,1,0:T(8,128)(2,1)S(1)} all-to-all(bf16[8,64,256]{2,1,0:T(8,128)(2,1)S(1)} %stack.5), channel_id=1, replica_groups=mesh['group'=2,'dp'=16,'tensor'=8] {'tensor'}, dimensions={0} | all-to-all | bytes 524288 | tf_op jit(solution)/shard_map/all_to_all | solution.py:20
  392.9 2.7 fusion.36
  395.7 1.1 fusion.35
  396.8 5.5 pad_maximum_fusion
  402.4 115.1 %reduce-scatter.9.cloned.1.call-done = f32[16,7168]{1,0:T(8,128)} async-done(((f32[512,7168]{1,0:T(8,128)}), f32[16,7168]{1,0:T(8,128)}) %reduce-scatter.9.cloned.1.call-update) | async-done | bytes 458768 | tf_op jit(solution)/shard_map/reduce_scatter | solution.py:22
  517.5 1.8 fusion.10
  519.3 50.4 %all-gather.4.cloned.1.call-done = bf16[512,3584]{1,0:T(8,128)(2,1)} async-done(((bf16[16,3584]{1,0:T(8,128)(2,1)}), bf16[512,3584]{1,0:T(8,128)(2,1)}) %all-gather.4.cloned.1.call-update) | async-done | bytes 3670032 | tf_op jit(solution)/shard_map/all_gather | solution.py:35
  569.7 4.5 fusion.37
  574.2 37.7 %reduce-scatter.11.cloned.1.call-done = f32[64,256]{1,0:T(8,128)} async-done(((f32[512,256]{1,0:T(8,128)}), f32[64,256]{1,0:T(8,128)}) %reduce-scatter.11.cloned.1.call-update) | async-done | bytes 65552 | tf_op jit(solution)/shard_map/reduce_scatter | solution.py:39
  612.0 1.5 fusion.19
  (46 shorter events, 0.8 us)
Async XLA Ops:
  6.5 181.7 %copy-start = (bf16[16,1,256,256]{3,2,1,0:T(8,128)(2,1)S(1)}, bf16[16,1,256,256]{3,2,1,0:T(8,128)(2,1)}, u32[]{:S(2)}) copy-start(bf16[16,1,256,256]{3,2,1,0:T(8,128)(2,1)} %param.21) | copy-start | bytes 6291460
  6.5 173.6 %reduce-scatter.5.cloned.1.call-start = ((), (), s32[]{:S(2)}) async-start(), calls=%async_computation.10 | async-start | bytes 2703360 | tf_op jit(solution)/shard_map/reduce_scatter | solution.py:22
  91.1 1.8 copy-start.6
  91.1 21.5 %copy-start.1 = (s32[16]{0:T(128)S(1)}, s32[16]{0:T(128)}, u32[]{:S(2)}) copy-start(s32[16]{0:T(128)} %param.22) | copy-start | bytes 196
  182.3 12.7 %all-to-all-start.3 = ((bf16[32,2,256]{2,1,0:T(2,128)(2,1)}), bf16[32,2,256]{2,1,0:T(2,128)(2,1)S(1)}, u32[]{:S(2)}, u32[]{:S(2)}) async-start(bf16[32,2,256]{2,1,0:T(2,128)(2,1)} %reshape.158), calls=%async_computation.4 | async-start | bytes 65536 | tf_op jit(solution)/shard_map/all_to_all | solution.py:118
  195.1 13.7 %all-to-all-start.2 = ((bf16[32,2,1024]{2,1,0:T(2,128)(2,1)}), bf16[32,2,1024]{2,1,0:T(2,128)(2,1)S(1)}, u32[]{:S(2)}, u32[]{:S(2)}) async-start(bf16[32,2,1024]{2,1,0:T(2,128)(2,1)} %reshape.155), calls=%async_computation.3 | async-start | bytes 262144 | tf_op jit(solution)/shard_map/all_to_all | solution.py:117
  212.9 63.0 %copy-start.5 = (bf16[1024,256]{1,0:T(8,128)(2,1)S(1)}, bf16[1024,256]{1,0:T(8,128)(2,1)}, u32[]{:S(2)}) copy-start(bf16[1024,256]{1,0:T(8,128)(2,1)} %param.17) | copy-start | bytes 1572868
  212.9 65.6 %copy-start.7 = (bf16[256]{0:T(256)(128)(2,1)S(1)}, bf16[256]{0:T(256)(128)(2,1)}, u32[]{:S(2)}) copy-start(bf16[256]{0:T(256)(128)(2,1)} %param.14) | copy-start | bytes 1540
  212.9 103.2 %copy-start.3 = (bf16[64,256]{1,0:T(8,128)(2,1)S(1)}, bf16[64,256]{1,0:T(8,128)(2,1)}, u32[]{:S(2)}) copy-start(bf16[64,256]{1,0:T(8,128)(2,1)} %param.12) | copy-start | bytes 98308
  216.6 11.7 %all-to-all-start.4 = ((bf16[32,2,1024]{2,1,0:T(2,128)(2,1)}), bf16[32,2,1024]{2,1,0:T(2,128)(2,1)S(1)}, u32[]{:S(2)}, u32[]{:S(2)}) async-start(bf16[32,2,1024]{2,1,0:T(2,128)(2,1)} %convert_element_type.59), calls=%async_computation.5 | async-start | bytes 262144 | tf_op jit(solution)/shard_map/all_to_all | solution.py:130
  221.8 54.0 %all-gather.6.cloned.1.call-start = ((), (), s32[]{:S(2)}) async-start(), calls=%async_computation.15 | async-start | bytes 1081344 | tf_op jit(solution)/shard_map/all_gather | solution.py:35
  229.5 86.5 %reduce-scatter.7.cloned.1.call-start = ((), (), s32[]{:S(2)}) async-start(), calls=%async_computation.11 | async-start | bytes 589824 | tf_op jit(solution)/shard_map/reduce_scatter | solution.py:39
  278.4 239.1 %reduce-scatter.9.cloned.1.call-start = ((), (), s32[]{:S(2)}) async-start(), calls=%async_computation.12 | async-start | bytes 15138816 | tf_op jit(solution)/shard_map/reduce_scatter | solution.py:22
  392.9 2.8 copy-start.2
  402.3 167.3 %all-gather.4.cloned.1.call-start = ((), (), s32[]{:S(2)}) async-start(), calls=%async_computation.13 | async-start | bytes 3784704 | tf_op jit(solution)/shard_map/all_gather | solution.py:35
  519.2 92.7 %copy-start.4 = (f32[64,256]{1,0:T(8,128)S(1)}, f32[64,256]{1,0:T(8,128)}, u32[]{:S(2)}) copy-start(f32[64,256]{1,0:T(8,128)} %reduce-scatter.7.cloned.1.call-done) | copy-start | bytes 196612
  519.2 92.7 %reduce-scatter.11.cloned.1.call-start = ((), (), s32[]{:S(2)}) async-start(), calls=%async_computation.14 | async-start | bytes 589824 | tf_op jit(solution)/shard_map/reduce_scatter | solution.py:39
Sparse Core Ops, SparseCore 0:
  93.0 87.1 reduce-scatter.4
  229.7 46.1 all-gather.5
  278.5 37.5 reduce-scatter.6
  402.5 114.9 reduce-scatter.8
  519.8 49.7 all-gather.3
  574.4 37.5 reduce-scatter.10
